TPU v7x, 256 devices: a whole 4x4x8 slice. The times are simulated.
256 devices in a mesh: branch: 2 (over z_hi), head: 4 (over x), page: 32 (over y, z_lo, core).
Axes of the slice: x: 4, y: 4, z: 8 (z_hi: 2, z_lo: 4; z = z_hi * 4 + z_lo), core: 2. Of those that a mesh axis runs over, the one named last changes fastest.
Arguments:
- queries: bfloat16 [16384, 4096], P(('branch', 'page'), 'head'), may hold values from -6 to 6
- new_keys: bfloat16 [16384, 512], P(('branch', 'page'), 'head'), may hold values from -6 to 6
- new_values: bfloat16 [16384, 512], P(('branch', 'page'), 'head'), may hold values from -6 to 6
- cache_keys: bfloat16 [128, 64, 512], P(('branch', 'page'), None, 'head'), may hold values from -6 to 6
- cache_values: bfloat16 [128, 64, 512], P(('branch', 'page'), None, 'head'), may hold values from -6 to 6
- block_table: int32 [64, 32], P(('branch', 'page')), may hold values from 0 to 127, as said below
- ancestor_len: int32 [64], P(('branch', 'page')), may hold values from 256 to 2048, as said below
- out_weight: bfloat16 [4096, 8192], P('head', 'page'), may hold values from -0.375 to 0.375
Outputs:
- layer_out: bfloat16 [16384, 8192], P(('branch', 'head'), 'page')
Inputs may be any that keep to these rules, and one draw needn't show every extreme that they name: `block_table`: each row names 32 distinct page ids; its first 4 entries are the same for every branch. `ancestor_len`: every branch's ancestors fill its first 4 pages; some branch reaches the maximum.
All inputs are finite; a program needn't handle non-finite values.
Results may differ from a plain program's by a relative error of at most 0.018.
Values may be sent and summed in bfloat16 or wider, within the bound.
No kernel may reach another device: no remote copies, remote signals or barrier semaphores. Data moves between devices by JAX's collectives and lax.ppermute only.
A program may use at most 64 MiB of HBM per device.

v0:
```python
import math
import jax
import jax.numpy as jnp
from jax import lax
from jax.sharding import PartitionSpec as P

HD = 128
PAGE_TOK = 64
NEW = 256
masked_fill = -1e30


def attend(carried, queries_here, key_block, value_block, usable, score_scale):
    running_max, running_sum, accumulated = carried
    scores = (
        jnp.einsum("kbnd,jkd->kbnj", queries_here, key_block, preferred_element_type=jnp.float32)
        * score_scale
    )
    key_mask = usable[None, :, None, :]
    block_max = jnp.max(jnp.where(key_mask, scores, masked_fill), axis=-1)
    new_max = jnp.maximum(running_max, block_max)
    shrink = jnp.exp(running_max - new_max)
    weights = jnp.where(key_mask, jnp.exp(scores - new_max[..., None]), 0.0).astype(jnp.bfloat16)
    running_sum = running_sum * shrink + jnp.sum(weights.astype(jnp.float32), axis=-1)
    accumulated = accumulated * shrink[..., None] + jnp.einsum(
        "kbnj,jkd->kbnd", weights, value_block, preferred_element_type=jnp.float32
    )
    return (new_max, running_sum, accumulated)


def shards(
    queries, new_keys, new_values, cache_keys, cache_values, block_table, ancestor_len, out_weight
):
    row_count = queries.shape[0]
    branches_here = block_table.shape[0]
    slot_count = block_table.shape[1]
    heads_here = queries.shape[1] // HD
    kv_here = new_keys.shape[1] // HD
    group_size = heads_here // kv_here
    query_span = NEW * group_size
    score_scale = 1.0 / math.sqrt(HD)
    queries_here = (
        queries.reshape(branches_here, NEW, kv_here, group_size, HD)
        .transpose(2, 0, 1, 3, 4)
        .reshape(kv_here, branches_here, query_span, HD)
    )
    own_keys = new_keys.reshape(row_count, kv_here, HD)
    own_values = new_values.reshape(row_count, kv_here, HD)
    token_index = (
        jnp.arange(branches_here, dtype=jnp.int32)[:, None] * NEW
        + jnp.arange(query_span, dtype=jnp.int32)[None, :] // group_size
    )
    key_index = jnp.arange(row_count, dtype=jnp.int32)
    own_mask = (key_index[None, None, :] // NEW == token_index[:, :, None] // NEW) & (
        key_index[None, None, :] <= token_index[:, :, None]
    )
    own_scores = (
        jnp.einsum("kbnd,jkd->kbnj", queries_here, own_keys, preferred_element_type=jnp.float32)
        * score_scale
    )
    start_max = jnp.max(jnp.where(own_mask[None], own_scores, masked_fill), axis=-1)
    own_weights = jnp.where(own_mask[None], jnp.exp(own_scores - start_max[..., None]), 0.0).astype(
        jnp.bfloat16
    )
    start_sum = jnp.sum(own_weights.astype(jnp.float32), axis=-1)
    start_acc = jnp.einsum(
        "kbnj,jkd->kbnd", own_weights, own_values, preferred_element_type=jnp.float32
    )
    slot_first = jnp.arange(slot_count, dtype=jnp.int32) * PAGE_TOK
    slot_limit = jnp.clip(ancestor_len[:, None] - slot_first[None, :], 0, PAGE_TOK)
    carried = (start_max, start_sum, start_acc)
    piece_keys = lax.all_gather(cache_keys, ("branch", "page"), axis=0, tiled=True)
    piece_values = lax.all_gather(cache_values, ("branch", "page"), axis=0, tiled=True)
    page_count = piece_keys.shape[0]
    page_ids = jnp.arange(page_count, dtype=jnp.int32)
    slot_hits = block_table[:, :, None] == page_ids[None, None, :]
    live_tokens = jnp.sum(jnp.where(slot_hits, slot_limit[:, :, None], 0), axis=1)
    usable = jnp.arange(PAGE_TOK, dtype=jnp.int32)[None, None, :] < live_tokens[:, :, None]
    key_total = page_count * PAGE_TOK
    block_len = math.gcd(key_total, 512)
    block_count = key_total // block_len
    key_blocks = piece_keys.reshape(block_count, block_len, kv_here, HD)
    value_blocks = piece_values.reshape(block_count, block_len, kv_here, HD)
    usable_blocks = usable.reshape(branches_here, block_count, block_len).transpose(1, 0, 2)

    def block_step(state, block_item):
        key_block, value_block, usable_block = block_item
        state = attend(state, queries_here, key_block, value_block, usable_block, score_scale)
        return (state, None)

    carried, _ = lax.scan(block_step, carried, (key_blocks, value_blocks, usable_blocks))
    final_max, final_sum, final_acc = carried
    attn_out = (final_acc / final_sum[..., None]).reshape(
        kv_here, branches_here, NEW, group_size, HD
    )
    attn_out = (
        attn_out.transpose(1, 2, 0, 3, 4).reshape(row_count, heads_here * HD).astype(jnp.bfloat16)
    )
    partial_term = jnp.dot(
        lax.all_gather(attn_out, "page", axis=0, tiled=True),
        out_weight,
        preferred_element_type=jnp.float32,
    ).astype(jnp.bfloat16)
    summed = lax.psum_scatter(
        partial_term.astype(jnp.float32).astype(jnp.bfloat16),
        "head",
        scatter_dimension=0,
        tiled=True,
    )
    return summed


def solution(mesh):
    in_specs = (
        P(("branch", "page"), "head"),
        P(("branch", "page"), "head"),
        P(("branch", "page"), "head"),
        P(("branch", "page"), None, "head"),
        P(("branch", "page"), None, "head"),
        P(("branch", "page"), None),
        P(("branch", "page")),
        P("head", "page"),
    )
    out_specs = P(("branch", "head"), "page")
    return jax.shard_map(shards, mesh=mesh, in_specs=in_specs, out_specs=out_specs, check_vma=False)
```

profile of v0, /device:TPU:1, one launch (start us, length us, event | category | flops | bytes accessed | tf_op | source)
XLA Modules:
  0.0 490.3 jit_solution(336189161934628019)
XLA Ops:
  15.0 112.1 %all-gather.4.cloned.1.call-done = bf16[128,64,128]{2,1,0:T(8,128)(2,1)} async-done(((bf16[2,64,128]{2,1,0:T(8,128)(2,1)}), bf16[128,64,128]{2,1,0:T(8,128)(2,1)}) %all-gather.4.cloned.1.call-update) | async-done | bytes 2097168 | tf_op jit(solution)/shard_map/all_gather | solution.py:72
  127.1 114.1 %all-gather.6.cloned.1.call-done = bf16[128,64,128]{2,1,0:T(8,128)(2,1)} async-done(((bf16[2,64,128]{2,1,0:T(8,128)(2,1)}), bf16[128,64,128]{2,1,0:T(8,128)(2,1)}) %all-gather.6.cloned.1.call-update) | async-done | bytes 2097168 | tf_op jit(solution)/shard_map/all_gather | solution.py:73
  241.2 80.6 %while.14 = (s32[]{:T(128)}, f32[1,1,2048]{2,1,0:T(1,128)S(1)}, f32[1,1,2048]{2,1,0:T(1,128)S(1)}, f32[1,1,2048,128]{3,2,1,0:T(8,128)S(1)}, pred[16,1,512]{2,0,1...) while((s32[]{:T(128)}, f32[1,1,2048]{2,1,0:T(1,128)S(1)}, ...), condition=%wide.region_6.7_spmd, body=%wide.region_3.6_spmd.sunk | while | flops 551030784 | bytes 15600241 | solution.py:91
  241.3 1.6 select_reduce_fusion.4
  243.8 2.4 fusion.24
  248.9 2.4 fusion.24
  251.3 1.6 select_reduce_fusion.4
  253.9 2.4 fusion.24
  258.9 2.4 fusion.24
  264.0 2.4 fusion.24
  269.0 2.4 fusion.24
  274.1 2.4 fusion.24
  279.1 2.4 fusion.24
  284.1 2.4 fusion.24
  289.2 2.4 fusion.24
  294.2 2.4 fusion.24
  299.2 2.4 fusion.24
  304.3 2.4 fusion.24
  309.3 2.4 fusion.24
  314.3 2.4 fusion.24
  319.4 2.4 fusion.24
  323.3 98.4 %all-gather.8.cloned.1.call-done = bf16[8192,1024]{1,0:T(8,128)(2,1)} async-done(((bf16[256,1024]{1,0:T(8,128)(2,1)}), bf16[8192,1024]{1,0:T(8,128)(2,1)}) %all-gather.8.cloned.1.call-update) | async-done | bytes 16777232 | tf_op jit(solution)/shard_map/all_gather | solution.py:100
  421.6 12.2 %convolution_convert_fusion = bf16[8192,256]{1,0:T(8,128)(2,1)} fusion(bf16[8192,1024]{1,0:T(8,128)(2,1)} %all-gather.8.cloned.1.call-done, bf16[1024,256]{1,0:T(8,128)(2,1)S(1)} %copy-done), kind=kOutput, calls=%fused_computation.16 | convolution fusion | flops 4297064448 | bytes 21495808 | tf_op jit(solution)/shard_map/dot_general | solution.py:99
  433.9 49.9 %reduce-scatter.2.cloned.1.call-done = bf16[2048,256]{1,0:T(8,128)(2,1)} async-done(((bf16[8192,256]{1,0:T(8,128)(2,1)}), bf16[2048,256]{1,0:T(8,128)(2,1)}) %reduce-scatter.2.cloned.1.call-update) | async-done | bytes 1048592 | tf_op jit(solution)/shard_map/reduce_scatter | solution.py:104
  (122 shorter events, 47.1 us)
Async XLA Ops:
  6.5 415.1 %copy-start = (bf16[1024,256]{1,0:T(8,128)(2,1)S(1)}, bf16[1024,256]{1,0:T(8,128)(2,1)}, u32[]{:S(2)}) copy-start(bf16[1024,256]{1,0:T(8,128)(2,1)} %param.17) | copy-start | bytes 1572868
  6.5 120.6 %all-gather.4.cloned.1.call-start = ((), (), s32[]{:S(2)}) async-start(), calls=%async_computation.1 | async-start | bytes 2129920 | tf_op jit(solution)/shard_map/all_gather | solution.py:72
  7.3 234.0 %all-gather.6.cloned.1.call-start = ((), (), s32[]{:S(2)}) async-start(), calls=%async_computation.2 | async-start | bytes 2129920 | tf_op jit(solution)/shard_map/all_gather | solution.py:73
  8.0 413.6 %all-gather.8.cloned.1.call-start = ((), (), s32[]{:S(2)}) async-start(), calls=%async_computation.3 | async-start | bytes 17301504 | tf_op jit(solution)/shard_map/all_gather | solution.py:100
  9.3 5.2 %copy-start.1 = (bf16[256,128]{1,0:T(8,128)(2,1)S(1)}, bf16[256,128]{1,0:T(8,128)(2,1)}, u32[]{:S(2)}) copy-start(bf16[256,128]{1,0:T(8,128)(2,1)} %param.12) | copy-start | bytes 196612
  323.2 160.6 %reduce-scatter.2.cloned.1.call-start = ((), (), s32[]{:S(2)}) async-start(), calls=%async_computation.4 | async-start | bytes 5242880 | tf_op jit(solution)/shard_map/reduce_scatter | solution.py:104
Sparse Core Ops, SparseCore 0:
  9.2 117.8 all-gather.3
  129.0 112.2 all-gather.5
  323.3 98.2 all-gather.7
  434.0 49.7 reduce-scatter.1
where the time goes:
time: 491 us; the launch traced here: 490 us
  waiting for transfers between devices  376 us (77%)
  matrix products  79 us (16%)
  other arithmetic  16.3 us (3%)
  between operations  13.8 us (3%)
    all_gather x1, waiting for transfers between devices, shards(): lax.all_gather(cache_values, ('branch', 'page'), axis=0, tiled=True)  114 us
    all_gather x1, waiting for transfers between devices, shards(): lax.all_gather(cache_keys, ('branch', 'page'), axis=0, tiled=True)  112 us
    all_gather x1, waiting for transfers between devices, shards(): lax.all_gather(attn_out, 'page', axis=0, tiled=True)  98.4 us
    reduce_scatter x1, waiting for transfers between devices, shards(): lax.psum_scatter(partial_term.astype(jnp.float32).astype(jnp.bfloat16), '...  49.9 us
    dot_general x16, matrix products, attend(): jnp.einsum('kbnj,jkd->kbnd', weights, value_block, preferred_element_type...  38.5 us
    dot_general x16, matrix products, attend(): jnp.einsum('kbnd,jkd->kbnj', queries_here, key_block, preferred_element_t...  26.3 us
    reduce_sum x16, other arithmetic, attend(): jnp.sum(weights.astype(jnp.float32), axis=-1)  13.8 us
    dot_general x1, matrix products, shards(): jnp.dot(lax.all_gather(attn_out, 'page', axis=0, tiled=True), out_weight,...  12.2 us
  transfers between devices with their start and end apart: 4, of which 4 were waited for; matrix products, arithmetic and copies ran while one was open for 1% of the time, Pallas kernels for 0%

commit v1 on v0

--- a/solution.py
+++ b/solution.py
@@ -8,6 +8,13 @@
 PAGE_TOK = 64
 NEW = 256
 masked_fill = -1e30
+
+
+def answer_heaps_here(obj, group_axis, dim_no):
+    current_value = lax.axis_size(group_axis)
+    r2 = jnp.stack([obj] * current_value)
+    n_now = lax.all_to_all(r2, concat_axis=0, split_axis=0, axis_name=group_axis)
+    return jnp.concatenate(n_now, axis=dim_no)
 
 
 def attend(carried, queries_here, key_block, value_block, usable, score_scale):
@@ -70,7 +77,7 @@
     slot_limit = jnp.clip(ancestor_len[:, None] - slot_first[None, :], 0, PAGE_TOK)
     carried = (start_max, start_sum, start_acc)
     piece_keys = lax.all_gather(cache_keys, ("branch", "page"), axis=0, tiled=True)
-    piece_values = lax.all_gather(cache_values, ("branch", "page"), axis=0, tiled=True)
+    piece_values = answer_heaps_here(cache_values, ("branch", "page"), 0)
     page_count = piece_keys.shape[0]
     page_ids = jnp.arange(page_count, dtype=jnp.int32)
     slot_hits = block_table[:, :, None] == page_ids[None, None, :]

time: 491 us -> 386 us (0.79)
  waiting for transfers between devices: 376 us -> 258 us
  starting transfers between devices: 0.12 us -> 13.6 us
    all_gather x1 -> x0, waiting for transfers between devices: 114 us -> none  [shards(): lax.all_gather(cache_values, ('branch', 'page'), axis=0, tiled=True)]
    all_to_all x0 -> x1, starting transfers between devices: none -> 13.3 us  [answer_heaps_here(): lax.all_to_all(r2, concat_axis=0, split_axis=0, axis_name=group_axis)]
  transfers between devices with their start and end apart: 4 -> 4, of which waited for: 4 -> 3; matrix products, arithmetic and copies ran while one was open for 1% -> 1% of each run, Pallas kernels for 0% -> 0%
where the time goes in v1:
time: 386 us; the launch traced here: 385 us
  waiting for transfers between devices  258 us (67%)
  matrix products  78.2 us (20%)
  other arithmetic  15.6 us (4%)
  between operations  13.9 us (4%)
  starting transfers between devices  13.6 us (4%)
  local copies, waits for them, and re-layouts  4.85 us (1%)
    all_gather x1, waiting for transfers between devices, shards(): lax.all_gather(cache_keys, ('branch', 'page'), axis=0, tiled=True)  107 us
    all_gather x1, waiting for transfers between devices, shards(): lax.all_gather(attn_out, 'page', axis=0, tiled=True)  100 us
    reduce_scatter x1, waiting for transfers between devices, shards(): lax.psum_scatter(partial_term.astype(jnp.float32).astype(jnp.bfloat16), '...  49.9 us
    dot_general x16, matrix products, attend(): jnp.einsum('kbnj,jkd->kbnd', weights, value_block, preferred_element_type...  38.5 us
    dot_general x16, matrix products, attend(): jnp.einsum('kbnd,jkd->kbnj', queries_here, key_block, preferred_element_t...  26.3 us
    reduce_sum x16, other arithmetic, attend(): jnp.sum(weights.astype(jnp.float32), axis=-1)  13.8 us
    all_to_all x1, starting transfers between devices, answer_heaps_here(): lax.all_to_all(r2, concat_axis=0, split_axis=0, axis_name=group_axis)  13.3 us
    dot_general x1, matrix products, shards(): jnp.dot(lax.all_gather(attn_out, 'page', axis=0, tiled=True), out_weight,...  12.2 us
  transfers between devices with their start and end apart: 4, of which 3 were waited for; matrix products, arithmetic and copies ran while one was open for 1% of the time, Pallas kernels for 0%

profile of v1, /device:TPU:1, one launch (start us, length us, event | category | flops | bytes accessed | tf_op | source)
XLA Modules:
  0.0 385.2 jit_solution(11456399077432349465)
XLA Ops:
  7.3 2.6 stack.2
  9.9 13.3 %all-to-all-start = ((bf16[64,2,64,128]{3,2,1,0:T(8,128)(2,1)}), bf16[64,2,64,128]{3,2,1,0:T(8,128)(2,1)}, u32[]{:S(2)}, u32[]{:S(2)}) async-start(bf16[64,2,64,128]{3,2,1,0:T(8,128)(2,1)} %stack.2), calls=%async_computation | async-start | bytes 4194304 | tf_op jit(solution)/shard_map/all_to_all | solution.py:16
  26.7 107.3 %all-gather.3.cloned.1.call-done = bf16[128,64,128]{2,1,0:T(8,128)(2,1)} async-done(((bf16[2,64,128]{2,1,0:T(8,128)(2,1)}), bf16[128,64,128]{2,1,0:T(8,128)(2,1)}) %all-gather.3.cloned.1.call-update) | async-done | bytes 2097168 | tf_op jit(solution)/shard_map/all_gather | solution.py:79
  134.0 80.6 %while.14 = (s32[]{:T(128)}, f32[1,1,2048]{2,1,0:T(1,128)S(1)}, f32[1,1,2048]{2,1,0:T(1,128)S(1)}, f32[1,1,2048,128]{3,2,1,0:T(8,128)S(1)}, pred[16,1,512]{2,0,1...) while((s32[]{:T(128)}, f32[1,1,2048]{2,1,0:T(1,128)S(1)}, ...), condition=%wide.region_6.7_spmd, body=%wide.region_3.6_spmd.sunk | while | flops 551030784 | bytes 15600241 | solution.py:98
  136.6 2.4 fusion.24
  139.1 1.6 select_reduce_fusion.4
  141.7 2.4 fusion.24
  146.7 2.4 fusion.24
  151.7 2.4 fusion.24
  156.8 2.4 fusion.24
  161.8 2.4 fusion.24
  166.8 2.4 fusion.24
  171.9 2.4 fusion.24
  176.9 2.4 fusion.24
  182.0 2.4 fusion.24
  187.0 2.4 fusion.24
  192.0 2.4 fusion.24
  197.1 2.4 fusion.24
  202.1 2.4 fusion.24
  207.1 2.4 fusion.24
  212.2 2.4 fusion.24
  216.2 100.3 %all-gather.5.cloned.1.call-done = bf16[8192,1024]{1,0:T(8,128)(2,1)} async-done(((bf16[256,1024]{1,0:T(8,128)(2,1)}), bf16[8192,1024]{1,0:T(8,128)(2,1)}) %all-gather.5.cloned.1.call-update) | async-done | bytes 16777232 | tf_op jit(solution)/shard_map/all_gather | solution.py:107
  316.5 12.2 %convolution_convert_fusion = bf16[8192,256]{1,0:T(8,128)(2,1)} fusion(bf16[8192,1024]{1,0:T(8,128)(2,1)} %all-gather.5.cloned.1.call-done, bf16[1024,256]{1,0:T(8,128)(2,1)S(1)} %copy-done), kind=kOutput, calls=%fused_computation.16 | convolution fusion | flops 4297064448 | bytes 21495808 | tf_op jit(solution)/shard_map/dot_general | solution.py:106
  328.8 49.9 %reduce-scatter.2.cloned.1.call-done = bf16[2048,256]{1,0:T(8,128)(2,1)} async-done(((bf16[8192,256]{1,0:T(8,128)(2,1)}), bf16[2048,256]{1,0:T(8,128)(2,1)}) %reduce-scatter.2.cloned.1.call-update) | async-done | bytes 1048592 | tf_op jit(solution)/shard_map/reduce_scatter | solution.py:111
  (128 shorter events, 44.6 us)
Async XLA Ops:
  6.5 310.0 %copy-start = (bf16[1024,256]{1,0:T(8,128)(2,1)S(1)}, bf16[1024,256]{1,0:T(8,128)(2,1)}, u32[]{:S(2)}) copy-start(bf16[1024,256]{1,0:T(8,128)(2,1)} %param.17) | copy-start | bytes 1572868
  6.5 16.8 %copy-start.1 = (bf16[256,1024]{1,0:T(8,128)(2,1)S(1)}, bf16[256,1024]{1,0:T(8,128)(2,1)}, u32[]{:S(2)}) copy-start(bf16[256,1024]{1,0:T(8,128)(2,1)} %param.10) | copy-start | bytes 1572868
  6.5 127.5 %all-gather.3.cloned.1.call-start = ((), (), s32[]{:S(2)}) async-start(), calls=%async_computation.2 | async-start | bytes 2129920 | tf_op jit(solution)/shard_map/all_gather | solution.py:79
  7.3 17.3 %copy-start.4 = (s32[1,32]{1,0:T(1,128)S(1)}, s32[1,32]{1,0:T(1,128)}, u32[]{:S(2)}) copy-start(s32[1,32]{1,0:T(1,128)} %param.15) | copy-start | bytes 388
  7.3 17.5 %copy-start.3 = (bf16[256,128]{1,0:T(8,128)(2,1)S(1)}, bf16[256,128]{1,0:T(8,128)(2,1)}, u32[]{:S(2)}) copy-start(bf16[256,128]{1,0:T(8,128)(2,1)} %param.11) | copy-start | bytes 196612
  9.9 124.1 %all-to-all-start = ((bf16[64,2,64,128]{3,2,1,0:T(8,128)(2,1)}), bf16[64,2,64,128]{3,2,1,0:T(8,128)(2,1)}, u32[]{:S(2)}, u32[]{:S(2)}) async-start(bf16[64,2,64,128]{3,2,1,0:T(8,128)(2,1)} %stack.2), calls=%async_computation | async-start | bytes 4194304 | tf_op jit(solution)/shard_map/all_to_all | solution.py:16
  23.3 293.2 %all-gather.5.cloned.1.call-start = ((), (), s32[]{:S(2)}) async-start(), calls=%async_computation.3 | async-start | bytes 17301504 | tf_op jit(solution)/shard_map/all_gather | solution.py:107
  23.5 2.7 copy-start.2
  216.0 162.7 %reduce-scatter.2.cloned.1.call-start = ((), (), s32[]{:S(2)}) async-start(), calls=%async_computation.4 | async-start | bytes 5242880 | tf_op jit(solution)/shard_map/reduce_scatter | solution.py:111
Sparse Core Ops, SparseCore 0:
  9.2 124.7 all-gather.2
  216.1 100.3 all-gather.4
  328.9 49.7 reduce-scatter.1
